TPU v7x, 512 devices: a whole 4x4x16 slice. The times are simulated.
512 devices in a mesh: day: 64 (over x, z_lo, core), pair: 8 (over y, z_hi).
Axes of the slice: x: 4, y: 4, z: 16 (z_hi: 2, z_lo: 8; z = z_hi * 8 + z_lo), core: 2. Of those that a mesh axis runs over, the one named last changes fastest.
Arguments:
- spectra: bfloat16 [256, 128, 1024], P('day', 'pair'), may hold values from -4 to 4
- pair_list: int32 [4096, 2], P('pair'), may hold values from 0 to 127, as said below
- mask: int32 [256, 128], P('day'), may hold values from 0 to 1
Outputs:
- linear_stack: float32 [401, 4096], P(None, ('pair', 'day'))
- weighted_stack: float32 [401, 4096], P(None, ('pair', 'day'))
Inputs may be any that keep to these rules, and one draw needn't show every extreme that they name: `pair_list`: the two stations of a pair differ.
All inputs are finite; a program needn't handle non-finite values.
Results may differ from a plain program's by a relative error of at most 0.0039.
Values may be sent and summed in bfloat16 or wider, within the bound.
No kernel may reach another device: no remote copies, remote signals or barrier semaphores. Data moves between devices by JAX's collectives and lax.ppermute only.
A program may use at most 64 MiB of HBM per device.

v0:
```python
import math
import jax
import jax.numpy as jnp
from jax import lax
from jax.sharding import PartitionSpec as P

F = 512
MAXLAG = 200
LAGS = 401


def lag_table():
    lag = jnp.arange(LAGS, dtype=jnp.int32) - MAXLAG
    freq = jnp.arange(F, dtype=jnp.int32)
    phase = jnp.mod(lag[:, None] * freq[None, :], 2 * F).astype(jnp.float32) * (math.pi / F)
    scale = 1.0 / math.sqrt(F)
    cosine = jnp.cos(phase) * scale
    sine = jnp.sin(phase) * scale
    upper = jnp.concatenate([cosine, -sine], 1)
    lower = jnp.concatenate([sine, cosine], 1)
    return jnp.concatenate([upper, lower], 0).astype(jnp.bfloat16)


def per_device(spectra, pair_list, mask):
    gathered = lax.all_gather(spectra, "pair", axis=1, tiled=True)
    station_count = gathered.shape[1]
    pair_rows = pair_list.shape[0]
    first = pair_list[:, 0]
    second = pair_list[:, 1]
    column = lax.broadcasted_iota(jnp.int32, (pair_rows, station_count), 1)
    pick_first = (first[:, None] == column).astype(jnp.float32)
    pick_second = (second[:, None] == column).astype(jnp.float32)
    mask_float = mask.astype(jnp.float32)
    weights = jnp.einsum("ds,ps->dp", mask_float, pick_first) * jnp.einsum(
        "ds,ps->dp", mask_float, pick_second
    )
    count_local = jnp.sum(weights, 0)[:, None]
    table = lag_table()

    def one_day(carry, inputs):
        day_spec, weight = inputs
        left = jnp.take(day_spec, first, axis=0).astype(jnp.float32)
        right = jnp.take(day_spec, second, axis=0).astype(jnp.float32)
        half = left.shape[1] // 2
        left_re, left_im = (left[:, :half], left[:, half:])
        right_re, right_im = (right[:, :half], right[:, half:])
        cross_re = left_re * right_re + left_im * right_im
        cross_im = left_im * right_re - left_re * right_im
        cross = jnp.concatenate([cross_re, cross_im], 1).astype(jnp.bfloat16)
        analytic = lax.dot_general(
            cross, table, (((1,), (1,)), ((), ())), preferred_element_type=jnp.float32
        )
        trace = analytic[:, :LAGS]
        hilbert = analytic[:, LAGS:]
        amplitude = jnp.sqrt(trace * trace + hilbert * hilbert)
        inverse = 1.0 / jnp.maximum(amplitude, 0.5)
        w = weight[:, None]
        lin_sum, real_sum, imag_sum = carry
        lin_sum = lin_sum + w * trace
        real_sum = real_sum + w * (trace * inverse)
        imag_sum = imag_sum + w * (hilbert * inverse)
        return ((lin_sum, real_sum, imag_sum), None)

    zeros = jnp.zeros((pair_rows, LAGS), jnp.float32)
    (lin_sum, real_sum, imag_sum), _ = lax.scan(one_day, (zeros, zeros, zeros), (gathered, weights))
    packed = jnp.concatenate([lin_sum, real_sum, imag_sum, count_local], 1)
    own = lax.psum_scatter(packed, "day", scatter_dimension=0, tiled=True)
    lin_own = own[:, :LAGS]
    real_own = own[:, LAGS : 2 * LAGS]
    imag_own = own[:, 2 * LAGS : 3 * LAGS]
    count_own = own[:, 3 * LAGS :]
    linear_stack = lin_own / count_own
    weighted_stack = (
        linear_stack * (real_own * real_own + imag_own * imag_own) / (count_own * count_own)
    )
    return (linear_stack.T, weighted_stack.T)


def solution(mesh):
    in_specs = (P("day", "pair", None), P("pair", None), P("day", None))
    out_specs = (P(None, ("pair", "day")), P(None, ("pair", "day")))
    return jax.shard_map(
        per_device, mesh=mesh, in_specs=in_specs, out_specs=out_specs, check_vma=False
    )
```

profile of v0, /device:TPU:16, one launch (start us, length us, event | category | flops | bytes accessed | tf_op | source)
XLA Modules:
  0.0 604.5 jit_solution(12339247741243256172)
XLA Ops:
  8.7 0.9 fusion.12
  9.7 1.0 fusion.23
  11.5 3.7 negate_convert_fusion
  15.2 1.4 maximum_maximum_fusion
  16.6 88.5 %all-gather.2.cloned.1.call-done = bf16[4,128,1024]{2,1,0:T(8,128)(2,1)} async-done(((bf16[4,16,1024]{2,1,0:T(8,128)(2,1)}), bf16[4,128,1024]{2,1,0:T(8,128)(2,1)}) %all-gather.2.cloned.1.call-update) | async-done | bytes 1048592 | tf_op jit(solution)/shard_map/all_gather | solution.py:25
  105.1 48.9 %while.15 = (s32[]{:T(128)}, f32[512,401]{0,1:T(8,128)}, f32[512,401]{0,1:T(8,128)}, f32[512,401]{0,1:T(8,128)}, f32[4,512]{1,0:T(4,128)S(1)}, /*index=5*/bf16[4...) while((s32[]{:T(128)}, f32[512,401]{0,1:T(8,128)}, ...), condition=%wide.region_1.3_spmd.clone, body=%wide.region_0.2_spmd.clone.sunk | while | flops 850545664 | bytes 46903560 | solution.py:65
  105.1 1.0 dynamic-slice_bitcast_fusion.2
  106.1 2.1 gather_fusion
  108.4 2.1 gather_fusion.1
  112.2 1.0 fusion.30
  113.6 1.8 select_add_fusion.4
  116.5 1.0 dynamic-slice_bitcast_fusion.2
  117.5 2.1 gather_fusion
  119.8 2.1 gather_fusion.1
  123.5 1.0 fusion.30
  124.9 2.9 select_add_fusion.4
  129.0 1.0 dynamic-slice_bitcast_fusion.2
  130.0 2.1 gather_fusion
  132.3 2.1 gather_fusion.1
  136.0 1.0 fusion.30
  137.4 2.9 select_add_fusion.4
  141.5 1.0 dynamic-slice_bitcast_fusion.2
  142.5 2.1 gather_fusion
  144.8 2.1 gather_fusion.1
  148.5 1.0 fusion.30
  149.9 2.9 select_add_fusion.4
  154.0 1.6 copy.10
  155.6 1.3 copy.8
  157.0 1.3 copy.9
  158.3 3.8 concatenate.22
  162.1 433.2 %reduce-scatter.2.cloned.1.call-done = f32[8,1204]{1,0:T(8,128)} async-done(((f32[512,1204]{1,0:T(8,128)}), f32[8,1204]{1,0:T(8,128)}) %reduce-scatter.2.cloned.1.call-update) | async-done | bytes 38544 | tf_op jit(solution)/shard_map/reduce_scatter | solution.py:67
  596.2 1.5 fusion.18
  (91 shorter events, 16.8 us)
Async XLA Ops:
  7.2 98.0 %all-gather.2.cloned.1.call-start = ((), (), s32[]{:S(2)}) async-start(), calls=%async_computation.1 | async-start | bytes 1179648 | tf_op jit(solution)/shard_map/all_gather | solution.py:25
  7.9 587.4 %reduce-scatter.2.cloned.1.call-start = ((), (), s32[]{:S(2)}) async-start(), calls=%async_computation.2 | async-start | bytes 2662400 | tf_op jit(solution)/shard_map/reduce_scatter | solution.py:67
  110.7 1.4 copy-start.7
  112.1 1.1 copy-start
  112.2 1.4 copy-start.3
  115.3 0.9 copy-start.1
  115.3 1.2 copy-start.4
  122.1 1.4 copy-start.7
  123.5 1.1 copy-start
  123.5 1.4 copy-start.3
  127.8 0.9 copy-start.1
  127.8 1.2 copy-start.4
  134.6 1.4 copy-start.7
  136.0 1.1 copy-start
  136.0 1.4 copy-start.3
  140.3 0.9 copy-start.1
  140.3 1.2 copy-start.4
  147.1 1.4 copy-start.7
  148.5 1.1 copy-start
  148.5 1.4 copy-start.3
  152.8 0.9 copy-start.1
  152.8 1.2 copy-start.4
  154.0 1.6 copy-start.2
  154.0 2.9 copy-start.5
  155.6 2.7 copy-start.8
  157.0 1.3 copy-start.6
Sparse Core Ops, SparseCore 0:
  11.2 93.8 all-gather.1
  162.2 433.0 reduce-scatter.1
where the time goes:
time: 605 us
  waiting for transfers between devices  522 us (86%)
  local copies, waits for them, and re-layouts  39.4 us (7%)
  other arithmetic  22.1 us (4%)
  between operations  14.1 us (2%)
  matrix products  6.06 us (1%)
    reduce_scatter x1, waiting for transfers between devices, per_device(): own = lax.psum_scatter(packed, 'day', scatter_dimension=0, tiled=True)  433 us
    all_gather x1, waiting for transfers between devices, per_device(): gathered = lax.all_gather(spectra, 'pair', axis=1, tiled=True)  88.5 us
  transfers between devices with their start and end apart: 2, of which 2 were waited for; matrix products, arithmetic and copies ran while one was open for 1% of the time, Pallas kernels for 0%

commit v1 on v0

--- a/solution.py
+++ b/solution.py
@@ -22,7 +22,9 @@
 
 
 def per_device(spectra, pair_list, mask):
-    gathered = lax.all_gather(spectra, "pair", axis=1, tiled=True)
+    gathered = jnp.concatenate(
+        lax.all_to_all(jnp.stack([spectra] * lax.axis_size("pair")), "pair", 0, 0), axis=1
+    )
     station_count = gathered.shape[1]
     pair_rows = pair_list.shape[0]
     first = pair_list[:, 0]

time: 605 us -> 585 us (0.967)
  the two profiles are of different devices: /device:TPU:16 before, /device:TPU:24 now
where the time goes in v1:
time: 585 us; the launch traced here: 584 us
  waiting for transfers between devices  483 us (83%)
  local copies, waits for them, and re-layouts  41.9 us (7%)
  other arithmetic  22 us (4%)
  starting transfers between devices  17.9 us (3%)
  between operations  14.1 us (2%)
    reduce_scatter x1, waiting for transfers between devices, per_device(): own = lax.psum_scatter(packed, 'day', scatter_dimension=0, tiled=True)  462 us
    all_to_all x1, waiting for transfers between devices, per_device(): lax.all_to_all(jnp.stack([spectra] * lax.axis_size('pair')), 'pair', 0, 0)  20.7 us
    all_to_all x1, starting transfers between devices, per_device(): lax.all_to_all(jnp.stack([spectra] * lax.axis_size('pair')), 'pair', 0, 0)  17.9 us
  transfers between devices with their start and end apart: 2, of which 2 were waited for; matrix products, arithmetic and copies ran while one was open for 1% of the time, Pallas kernels for 0%

profile of v1, /device:TPU:24, one launch (start us, length us, event | category | flops | bytes accessed | tf_op | source)
XLA Modules:
  0.0 584.1 jit_solution(8289647500224444459)
XLA Ops:
  7.2 2.0 stack.2
  9.2 17.9 %all-to-all-start = ((bf16[8,4,16,1024]{3,2,1,0:T(8,128)(2,1)}), bf16[8,4,16,1024]{3,2,1,0:T(8,128)(2,1)S(1)}, u32[]{:S(2)}, u32[]{:S(2)}) async-start(bf16[8,4,16,1024]{3,2,1,0:T(8,128)(2,1)} %stack.2), calls=%async_computation | async-start | bytes 2097152 | tf_op jit(solution)/shard_map/all_to_all | solution.py:26
  28.6 3.7 negate_convert_fusion
  32.3 1.4 maximum_maximum_fusion
  33.8 20.7 %all-to-all-done = bf16[8,4,16,1024]{3,2,1,0:T(8,128)(2,1)S(1)} async-done(((bf16[8,4,16,1024]{3,2,1,0:T(8,128)(2,1)}), bf16[8,4,16,1024]{3,2,1,0:T(8,128)(2,1)S(1)}, u32[]{:S(2)}, u32[]{:S(2)}) %all-to-all-start) | async-done | bytes 1048608 | tf_op jit(solution)/shard_map/all_to_all | solution.py:26
  54.5 1.1 copy.16
  55.6 48.9 %while.15 = (s32[]{:T(128)}, f32[512,401]{0,1:T(8,128)}, f32[512,401]{0,1:T(8,128)}, f32[512,401]{0,1:T(8,128)}, f32[4,512]{1,0:T(4,128)S(1)}, /*index=5*/bf16[4...) while((s32[]{:T(128)}, f32[512,401]{0,1:T(8,128)}, ...), condition=%wide.region_1.3_spmd.clone, body=%wide.region_0.2_spmd.clone.sunk | while | flops 850545664 | bytes 46903560 | solution.py:67
  55.6 1.0 dynamic-slice_bitcast_fusion.2
  56.5 2.1 gather_fusion
  58.9 2.1 gather_fusion.1
  62.6 1.0 fusion.30
  64.0 1.7 select_add_fusion.4
  66.9 1.0 dynamic-slice_bitcast_fusion.2
  67.9 2.1 gather_fusion
  70.2 2.1 gather_fusion.1
  73.9 1.0 fusion.30
  75.3 2.9 select_add_fusion.4
  79.4 1.0 dynamic-slice_bitcast_fusion.2
  80.4 2.1 gather_fusion
  82.7 2.1 gather_fusion.1
  86.4 1.0 fusion.30
  87.8 2.9 select_add_fusion.4
  92.9 2.1 gather_fusion
  95.2 2.1 gather_fusion.1
  98.9 1.0 fusion.30
  100.3 2.9 select_add_fusion.4
  104.4 1.6 copy.17
  106.0 1.3 copy.18
  107.4 1.3 copy.19
  108.7 3.9 concatenate.22
  112.6 462.3 %reduce-scatter.2.cloned.1.call-done = f32[8,1204]{1,0:T(8,128)} async-done(((f32[512,1204]{1,0:T(8,128)}), f32[8,1204]{1,0:T(8,128)}) %reduce-scatter.2.cloned.1.call-update) | async-done | bytes 38544 | tf_op jit(solution)/shard_map/reduce_scatter | solution.py:69
  575.8 1.5 fusion.18
  (96 shorter events, 16.8 us)
Async XLA Ops:
  7.2 20.0 %copy-start.9 = (s32[512,2]{0,1:T(2,128)S(1)}, s32[512,2]{0,1:T(2,128)}, u32[]{:S(2)}) copy-start(s32[512,2]{0,1:T(2,128)} %param.8) | copy-start | bytes 12292
  7.2 20.0 %copy-start.10 = (s32[4,128]{1,0:T(4,128)S(1)}, s32[4,128]{1,0:T(4,128)}, u32[]{:S(2)}) copy-start(s32[4,128]{1,0:T(4,128)} %param.9) | copy-start | bytes 6148
  9.2 45.3 %all-to-all-start = ((bf16[8,4,16,1024]{3,2,1,0:T(8,128)(2,1)}), bf16[8,4,16,1024]{3,2,1,0:T(8,128)(2,1)S(1)}, u32[]{:S(2)}, u32[]{:S(2)}) async-start(bf16[8,4,16,1024]{3,2,1,0:T(8,128)(2,1)} %stack.2), calls=%async_computation | async-start | bytes 2097152 | tf_op jit(solution)/shard_map/all_to_all | solution.py:26
  27.2 547.7 %reduce-scatter.2.cloned.1.call-start = ((), (), s32[]{:S(2)}) async-start(), calls=%async_computation.2 | async-start | bytes 2662400 | tf_op jit(solution)/shard_map/reduce_scatter | solution.py:69
  61.1 1.4 copy-start.7
  62.6 1.1 copy-start
  62.6 1.4 copy-start.2
  65.7 0.9 copy-start.1
  65.7 1.2 copy-start.3
  72.5 1.4 copy-start.7
  73.9 1.1 copy-start
  73.9 1.4 copy-start.2
  78.2 0.9 copy-start.1
  78.2 1.2 copy-start.3
  85.0 1.4 copy-start.7
  86.4 1.1 copy-start
  86.4 1.4 copy-start.2
  90.7 0.9 copy-start.1
  90.7 1.2 copy-start.3
  97.5 1.4 copy-start.7
  98.9 1.1 copy-start
  98.9 1.4 copy-start.2
  103.2 0.9 copy-start.1
  103.2 1.2 copy-start.3
  104.4 1.6 copy-start.4
  104.4 3.0 copy-start.5
  106.0 2.7 copy-start.8
  107.4 1.3 copy-start.6
Sparse Core Ops, SparseCore 0:
  112.7 462.1 reduce-scatter.1
